TPU v7x, 32 devices: a whole 2x2x4 slice. The times are simulated.
32 devices in a mesh: grp: 4 (over y, x), dev: 8 (over z, core).
Axes of the slice: x: 2, y: 2, z: 4, core: 2. Of those that a mesh axis runs over, the one named last changes fastest.
Arguments:
- panel_nodes: float32 [3, 262144], P(None, ('grp', 'dev')), may hold values from -1.6 to 1.6, as said below
- density: float32 [262144], P(('grp', 'dev')), may hold values from -6 to 6
- crevice_routes: int32 [16384, 2], P(('grp', 'dev')), may hold values from 0 to 31, all different within a row; in each aligned block of 512 rows (0 to 511, 512 to 1023, ...) at most 64 rows name the same one
- crevice_centre: int32 [16384, 2], P(('grp', 'dev')), may hold values from 0 to 511
- centres: float32 [3, 16384], P(None, ('grp', 'dev')), may hold values from -0.3 to 0.3, as said below
- targets: float32 [3, 262144], P(None, ('grp', 'dev')), may hold values from -0.8 to 0.8, as said below
- centre_home: int32 [16384, 1], P(('grp', 'dev')), may hold values from 0 to 31; in each aligned block of 512 rows (0 to 511, 512 to 1023, ...) at most 32 rows name the same one
- upsample: float32 [64, 16], replicated, may hold values from 0 to 1, as said below
- fine_weights: float32 [64], replicated, may hold values from 0.005 to 0.05
Outputs:
- returned: float32 [524288], P(('grp', 'dev'))
Inputs may be any that keep to these rules, and one draw needn't show every extreme that they name: `crevice_routes`: each device's 512 panels name at most 64 (panel, route) pairs for any one owner device, and some owner reaches 64 in every draw; the 2 owners of one panel differ. `centre_home`: among the 512 centres of one device at most 32 have the same home, and that bound is reached in every draw; entries of returned with no centre are zero. `panel_nodes`: every point in the convex hull of one panel's nodes lies at distance 0.9 or more from the anchor; every panel node lies within 1.6 of the anchor. `centres`: every centre lies within 0.3 of the anchor. `targets`: each target node lies at distance 0.3 to 0.5 from its centre. `upsample`: entries are positive and each row sums to one.
All inputs are finite; a program needn't handle non-finite values.
Results may differ from a plain program's by a relative error of at most 0.0003.
Values sent between devices are 32-bit elements; how exact they have to be, the bound alone decides.
No kernel may reach another device: no remote copies, remote signals or barrier semaphores. Data moves between devices by JAX's collectives and lax.ppermute only.
A program may use at most 64 MiB of HBM per device.

v0:
```python
import jax
import jax.numpy as jnp
from jax import lax
from jax.sharding import PartitionSpec as P

ORDER = 8
HI = lax.Precision.HIGHEST


def route_rank(destination, count):
    rows = destination.shape[0]
    onehot = (destination[:, None] == jnp.arange(count, dtype=jnp.int32)[None, :]).astype(
        jnp.bfloat16
    )
    lower = (jnp.arange(rows)[:, None] > jnp.arange(rows)[None, :]).astype(jnp.bfloat16)
    before = jnp.dot(lower, onehot, preferred_element_type=jnp.float32)
    return jnp.sum(before * onehot.astype(jnp.float32), axis=1).astype(jnp.int32)


def expansion_terms(fine, strength, centre_pos, rel_targets):
    src = fine - centre_pos[:, None, :]
    rs2 = jnp.sum(src * src, axis=0)
    rt2 = jnp.sum(rel_targets * rel_targets, axis=0)
    inv_rs2 = 1.0 / rs2
    scale = strength * lax.rsqrt(rs2)
    inner = jnp.sum(src[:, :, None, :] * rel_targets[:, None, :, :], axis=0)
    w = inner * inv_rs2[:, None, :]
    rho2 = rt2[None, :, :] * inv_rs2[:, None, :]
    p_prev = jnp.ones_like(w)
    p_now = w
    total = 1.0 + w
    for level in range(1, ORDER):
        p_next = (2 * level + 1) / (level + 1) * w * p_now - level / (level + 1) * rho2 * p_prev
        total = total + p_next
        p_prev, p_now = (p_now, p_next)
    return jnp.sum(scale[:, None, :] * total, axis=0)


def per_device(
    panel_nodes,
    density,
    crevice_routes,
    crevice_centre,
    centres,
    targets,
    centre_home,
    upsample,
    fine_weights,
):
    devices = lax.axis_size(("grp", "dev"))
    panels = crevice_routes.shape[0]
    fanout = crevice_routes.shape[1]
    centre_count = centres.shape[1]
    capacity = max(2, 2 * panels * fanout // devices)
    capacity_back = max(2, 2 * centre_count // devices)
    fine_count, nodes = upsample.shape
    pairs = panels * fanout
    slots = devices * capacity
    coarse = jnp.concatenate(
        [
            panel_nodes.reshape(3, panels, nodes).transpose(0, 2, 1).reshape(3 * nodes, panels),
            density.reshape(panels, nodes).T,
        ],
        axis=0,
    )
    coarse_pairs = jnp.repeat(coarse, fanout, axis=1)
    ids_pairs = (crevice_centre.reshape(1, pairs) + 1).astype(jnp.float32)
    payload = jnp.concatenate([coarse_pairs, ids_pairs], axis=0)
    destination = crevice_routes.reshape(-1)
    slot_index = destination * capacity + route_rank(destination, devices)
    place = (slot_index[:, None] == jnp.arange(slots, dtype=jnp.int32)[None, :]).astype(jnp.float32)
    outgoing = jnp.dot(payload, place, precision=HI)
    incoming = lax.all_to_all(outgoing, ("grp", "dev"), split_axis=1, concat_axis=1, tiled=True)
    ids = jnp.round(incoming[4 * nodes]).astype(jnp.int32) - 1
    valid = ids >= 0
    pick = (ids[:, None] == jnp.arange(centre_count, dtype=jnp.int32)[None, :]).astype(jnp.float32)
    centre_pos = centres
    rel = targets.reshape(3, centre_count, nodes) - centre_pos[:, :, None]
    centre_data = jnp.concatenate(
        [centre_pos, rel.transpose(0, 2, 1).reshape(3 * nodes, centre_count)], axis=0
    )
    gathered = lax.dot_general(centre_data, pick, (((1,), (1,)), ((), ())), precision=HI)
    slot_centre = gathered[:3]
    slot_targets = gathered[3:].reshape(3, nodes, slots)
    coarse_in = incoming[: 4 * nodes].reshape(4, nodes, slots)
    upper = jnp.einsum("jn,cns->cjs", upsample, coarse_in, precision=HI)
    strength = upper[3] * fine_weights[:, None]
    terms = expansion_terms(upper[:3], strength, slot_centre, slot_targets)
    terms = jnp.where(valid[None, :], terms, 0.0)
    potential = jnp.dot(terms, pick, precision=HI)
    home = centre_home.reshape(-1)
    back_index = home * capacity_back + route_rank(home, devices)
    back_place = (
        back_index[None, :] == jnp.arange(devices * capacity_back, dtype=jnp.int32)[:, None]
    ).astype(jnp.float32)
    sending = lax.dot_general(back_place, potential, (((1,), (1,)), ((), ())), precision=HI)
    sending = sending.reshape(devices, capacity_back * nodes)
    returned = lax.all_to_all(sending, ("grp", "dev"), split_axis=0, concat_axis=0, tiled=True)
    return returned.reshape(-1)


def solution(mesh):
    placed = (
        P(None, ("grp", "dev")),
        P(("grp", "dev")),
        P(("grp", "dev"), None),
        P(("grp", "dev"), None),
        P(None, ("grp", "dev")),
        P(None, ("grp", "dev")),
        P(("grp", "dev"), None),
        P(),
        P(),
    )
    return jax.shard_map(
        per_device, mesh=mesh, in_specs=placed, out_specs=P(("grp", "dev")), check_vma=False
    )
```

profile of v0, /device:TPU:0, one launch (start us, length us, event | category | flops | bytes accessed | tf_op | source)
XLA Modules:
  0.0 91.0 jit_solution(11559862471947307797)
XLA Ops:
  0.0 0.7 add_convert_fusion
  1.1 0.9 reshape.130
  2.0 0.8 copy.45
  3.1 0.5 fusion.26
  3.6 1.2 %reshape.128 = f32[3,512,16]{2,1,0:T(8,128)S(1)} reshape(f32[3,8192]{1,0:T(4,128)} %param.9) | data formatting | bytes 196608 | tf_op jit(solution)/shard_map/reshape | solution.py:61
  4.8 0.2 copy.40
  5.4 8.0 %fusion.17 = f32[65,2048]{0,1:T(8,128)} fusion(s32[1024]{0:T(1024)S(1)} %convert_add_fusion, f32[1,1024]{0,1:T(8,128)S(1)} %convert_element_type.66, f32[64,1024]{0,1:T(8,128)S(1)} %bitcast.29), kind=kOutput, calls=%fused_computation.27 | convolution fusion | flops 1637942272 | bytes 802816 | tf_op jit(solution)/shard_map/all_to_all | solution.py:73
  13.4 7.5 %all-to-all-start = ((f32[65,32,64]{0,2,1:T(8,128)}), f32[65,32,64]{0,2,1:T(8,128)S(1)}, u32[]{:S(2)}, u32[]{:S(2)}) async-start(f32[65,32,64]{0,2,1:T(8,128)} %bitcast.5), calls=%async_computation | async-start | bytes 2097152 | tf_op jit(solution)/shard_map/all_to_all | solution.py:73
  20.9 0.3 reshape.134
  21.2 0.3 subtract_bitcast_fusion
  21.7 0.3 fusion.27
  22.0 26.3 %all-to-all-done = f32[65,32,64]{0,2,1:T(8,128)S(1)} async-done(((f32[65,32,64]{0,2,1:T(8,128)}), f32[65,32,64]{0,2,1:T(8,128)S(1)}, u32[]{:S(2)}, u32[]{:S(2)}) %all-to-all-start) | async-done | bytes 532512 | tf_op jit(solution)/shard_map/all_to_all | solution.py:73
  48.3 0.9 fusion.30
  49.3 2.2 %fusion.19 = f32[51,2048]{1,0:T(8,128)S(1)} fusion(s32[2048]{0:T(1024)S(1)} %sub.44, f32[48,512]{1,0:T(8,128)S(1)} %bitcast.33, f32[3,512]{1,0:T(4,128)S(1)} %copy-done.2), kind=kOutput, calls=%fused_computation.30 | convolution fusion | flops 642803200 | bytes 530432 | tf_op jit(solution)/shard_map/dot_general | solution.py:82
  51.6 0.9 %copy.47 = f32[64,32,64]{2,1,0:T(8,128)S(1)} copy(f32[64,32,64]{0,2,1:T(8,128)S(1)} %bitcast.25) | data formatting | bytes 1048576 | tf_op jit(solution)/shard_map/slice | solution.py:85
  52.5 0.4 reshape.133
  52.9 1.9 %convolution_bitcast_fusion = f32[4,64,2048]{2,1,0:T(8,128)S(1)} fusion(f32[4,16,2048]{2,1,0:T(8,128)S(1)} %reshape.133, f32[64,16]{0,1:T(8,128)S(1)} %copy-done), kind=kOutput, calls=%fused_computation.34 | convolution fusion | flops 100663296 | bytes 2625536 | tf_op jit(solution)/shard_map/jn,cns->cjs/dot_general | solution.py:86
  54.8 1.5 %multiply_reduce_fusion.1 = (f32[64,2048]{1,0:T(8,128)S(1)}, f32[3,64,2048]{2,1,0:T(8,128)}) fusion(f32[3,2048]{1,0:T(4,128)S(1)} %slice.30, f32[4,64,2048]{2,1,0:T(8,128)S(1)} %convolution_bitcast_fusion), kind=kLoop, calls=%fused_computation.40 | loop fusion | flops 1048576 | bytes 3694592 | tf_op jit(solution)/shard_map/reduce_sum | solution.py:22
  56.3 7.7 %multiply_reduce_fusion = f32[64,16,2048]{2,1,0:T(8,128)} fusion(f32[3,16,2048]{2,1,0:T(8,128)S(1)} %bitcast.27, f32[3,64,2048]{2,1,0:T(8,128)} %get-tuple-element.6), kind=kLoop, calls=%fused_computation.7 | loop fusion | flops 10485760 | bytes 10354688 | tf_op jit(solution)/shard_map/reduce_sum | solution.py:26
  64.1 14.1 %fusion.15 = f32[16,2048]{1,0:T(8,128)S(1)} fusion(f32[64,16,2048]{2,1,0:T(8,128)} %multiply_reduce_fusion, f32[16,2048]{1,0:T(8,128)S(1)} %multiply_reduce_fusion.2, f32[64,2048]{1,0:T(8,128)S(1)} %get-tuple-element.8, f32[64,2048]{1,0:T(8,128)S(1)} %get-tuple-element.7), kind=kLoop, calls=%fused_computation.24 | loop fusion | flops 96436224 | bytes 9699328 | tf_op jit(solution)/shard_map/reduce_sum | solution.py:36
  78.2 1.4 %fusion.18 = f32[16,512]{1,0:T(8,128)S(1)} fusion(s32[2048]{0:T(1024)S(1)} %sub.44, f32[16,2048]{1,0:T(8,128)S(1)} %fusion.15, pred[2048]{0:T(1024)(128)(4,1)S(1)} %broadcast_compare_fusion), kind=kOutput, calls=%fused_computation.29 | convolution fusion | flops 202407936 | bytes 174080 | tf_op jit(solution)/shard_map/dot_general | solution.py:90
  79.7 1.0 %fusion.24 = f32[1024,16]{1,0:T(8,128)S(1)} fusion(f32[16,512]{1,0:T(8,128)S(1)} %fusion.18, s32[512]{0:T(512)S(1)} %convert_add_fusion.1), kind=kOutput, calls=%fused_computation.38 | convolution fusion | flops 101187584 | bytes 100352 | tf_op jit(solution)/shard_map/dot_general | solution.py:96
  80.9 9.4 %all_to_all.19 = f32[32,1,512]{2,1,0:T(1,128)S(1)} all-to-all(f32[32,1,512]{2,1,0:T(1,128)S(1)} %all_to_all.16), channel_id=1, replica_groups=mesh['grp'=4,'dev'=8] {'grp','dev'}, dimensions={0} | all-to-all | bytes 131072 | tf_op jit(solution)/shard_map/all_to_all | solution.py:98
  90.3 0.6 copy.54
  (27 shorter events, 1.7 us)
Async XLA Ops:
  0.0 52.9 %copy-start = (f32[64,16]{0,1:T(8,128)S(1)}, f32[64,16]{0,1:T(8,128)}, u32[]{:S(2)}) copy-start(f32[64,16]{0,1:T(8,128)} %param.16) | copy-start | bytes 12292
  0.0 20.9 %copy-start.1 = (f32[3,8192]{1,0:T(4,128)S(1)}, f32[3,8192]{1,0:T(4,128)}, u32[]{:S(2)}) copy-start(f32[3,8192]{1,0:T(4,128)} %param.14) | copy-start | bytes 294916
  0.0 21.1 %copy-start.2 = (f32[3,512]{1,0:T(4,128)S(1)}, f32[3,512]{1,0:T(4,128)}, u32[]{:S(2)}) copy-start(f32[3,512]{1,0:T(4,128)} %param.13) | copy-start | bytes 18436
  0.0 21.7 %copy-start.3 = (s32[512,1]{0,1:T(1,128)S(1)}, s32[512,1]{0,1:T(1,128)}, u32[]{:S(2)}) copy-start(s32[512,1]{0,1:T(1,128)} %param.15) | copy-start | bytes 6148
  13.4 34.9 %all-to-all-start = ((f32[65,32,64]{0,2,1:T(8,128)}), f32[65,32,64]{0,2,1:T(8,128)S(1)}, u32[]{:S(2)}, u32[]{:S(2)}) async-start(f32[65,32,64]{0,2,1:T(8,128)} %bitcast.5), calls=%async_computation | async-start | bytes 2097152 | tf_op jit(solution)/shard_map/all_to_all | solution.py:73
  52.9 11.1 %copy-start.4 = (f32[64]{0:T(128)S(1)}, f32[64]{0:T(128)}, u32[]{:S(2)}) copy-start(f32[64]{0:T(128)} %param.17) | copy-start | bytes 772
where the time goes:
time: 91.4 us; the launch traced here: 91 us
  waiting for transfers between devices  26.3 us (29%)
  other arithmetic  25.4 us (28%)
  matrix products  15.4 us (17%)
  blocking collectives  9.41 us (10%)
  starting transfers between devices  7.49 us (8%)
  local copies, waits for them, and re-layouts  6.79 us (7%)
    all_to_all x1, waiting for transfers between devices, per_device(): lax.all_to_all(outgoing, ('grp', 'dev'), split_axis=1, concat_axis=1, til...  26.3 us
    reduce_sum x1, other arithmetic, expansion_terms(): return jnp.sum(scale[:, None, :] * total, axis=0)  14.1 us
    all_to_all x1, blocking collectives, per_device(): lax.all_to_all(sending, ('grp', 'dev'), split_axis=0, concat_axis=0, tile...  9.41 us
    all_to_all x1, matrix products, per_device(): lax.all_to_all(outgoing, ('grp', 'dev'), split_axis=1, concat_axis=1, til...  7.97 us
    reduce_sum x1, other arithmetic, expansion_terms(): inner = jnp.sum(src[:, :, None, :] * rel_targets[:, None, :, :], axis=0)  7.67 us
    all_to_all x1, starting transfers between devices, per_device(): lax.all_to_all(outgoing, ('grp', 'dev'), split_axis=1, concat_axis=1, til...  7.49 us
    dot_general x1, matrix products, per_device(): lax.dot_general(centre_data, pick, (((1,), (1,)), ((), ())), precision=HI)  2.24 us
    dot_general x1, matrix products, per_device(): upper = jnp.einsum('jn,cns->cjs', upsample, coarse_in, precision=HI)  1.89 us
  transfers between devices with their start and end apart: 1, of which 1 were waited for; matrix products, arithmetic and copies ran while one was open for 1% of the time, Pallas kernels for 0%

commit v1 on v0

--- a/solution.py
+++ b/solution.py
@@ -5,6 +5,14 @@
 
 ORDER = 8
 HI = lax.Precision.HIGHEST
+
+
+def strings_guide(vector):
+    g_now = lax.axis_size(("grp", "dev"))
+    near = jnp.split(vector, g_now, 1)
+    big = jnp.stack(near, 0)
+    e_next = lax.all_to_all(big, ("grp", "dev"), 0, 0)
+    return jnp.concatenate(e_next, 1)
 
 
 def route_rank(destination, count):
@@ -70,7 +78,7 @@
     slot_index = destination * capacity + route_rank(destination, devices)
     place = (slot_index[:, None] == jnp.arange(slots, dtype=jnp.int32)[None, :]).astype(jnp.float32)
     outgoing = jnp.dot(payload, place, precision=HI)
-    incoming = lax.all_to_all(outgoing, ("grp", "dev"), split_axis=1, concat_axis=1, tiled=True)
+    incoming = strings_guide(outgoing)
     ids = jnp.round(incoming[4 * nodes]).astype(jnp.int32) - 1
     valid = ids >= 0
     pick = (ids[:, None] == jnp.arange(centre_count, dtype=jnp.int32)[None, :]).astype(jnp.float32)

time: 91.4 us -> 88.2 us (0.965)
  matrix products: 15.4 us -> 10.8 us
  local copies, waits for them, and re-layouts: 6.79 us -> 8.95 us
    all_to_all x1 -> x0, matrix products: 7.97 us -> none  [per_device(): lax.all_to_all(outgoing, ('grp', 'dev'), split_axis=1, concat_axis=1, til...]
    dot_general x0 -> x1, matrix products: none -> 3.42 us  [per_device(): outgoing = jnp.dot(payload, place, precision=HI)]
    unnamed x12 -> x51, local copies, waits for them, and re-layouts: 1.49 us -> 3.84 us
    another operation x0 -> x2, local copies, waits for them, and re-layouts: none -> 1.48 us  [strings_guide(): big = jnp.stack(near, 0)]
where the time goes in v1:
time: 88.2 us; the launch traced here: 87.8 us
  waiting for transfers between devices  26.1 us (30%)
  other arithmetic  24.7 us (28%)
  matrix products  10.8 us (12%)
  blocking collectives  9.41 us (11%)
  local copies, waits for them, and re-layouts  8.95 us (10%)
  starting transfers between devices  7.48 us (8%)
    all_to_all x1, waiting for transfers between devices, strings_guide(): e_next = lax.all_to_all(big, ('grp', 'dev'), 0, 0)  26.1 us
    reduce_sum x1, other arithmetic, expansion_terms(): return jnp.sum(scale[:, None, :] * total, axis=0)  14.1 us
    all_to_all x1, blocking collectives, per_device(): lax.all_to_all(sending, ('grp', 'dev'), split_axis=0, concat_axis=0, tile...  9.41 us
    reduce_sum x1, other arithmetic, expansion_terms(): inner = jnp.sum(src[:, :, None, :] * rel_targets[:, None, :, :], axis=0)  7.67 us
    all_to_all x1, starting transfers between devices, strings_guide(): e_next = lax.all_to_all(big, ('grp', 'dev'), 0, 0)  7.48 us
    unnamed x51, local copies, waits for them, and re-layouts  3.84 us
    dot_general x1, matrix products, per_device(): outgoing = jnp.dot(payload, place, precision=HI)  3.42 us
    dot_general x1, matrix products, per_device(): lax.dot_general(centre_data, pick, (((1,), (1,)), ((), ())), precision=HI)  2.23 us
  transfers between devices with their start and end apart: 1, of which 1 were waited for; matrix products, arithmetic and copies ran while one was open for 1% of the time, Pallas kernels for 0%

profile of v1, /device:TPU:0, one launch (start us, length us, event | category | flops | bytes accessed | tf_op | source)
XLA Modules:
  0.0 87.8 jit_solution(3625277085427249034)
XLA Ops:
  0.0 0.9 copy.46
  1.0 0.5 fusion.26
  1.6 0.3 reshape.131
  1.9 0.2 copy.41
  3.3 3.4 %fusion.17 = f32[65,2048]{1,0:T(8,128)S(1)} fusion(s32[1024]{0:T(1024)S(1)} %convert_add_fusion, f32[1,1024]{0,1:T(8,128)S(1)} %convert_element_type.66, f32[64,1024]{0,1:T(8,128)S(1)} %bitcast.158), kind=kOutput, calls=%fused_computation.27 | convolution fusion | flops 1637942272 | bytes 802816 | tf_op jit(solution)/shard_map/dot_general | solution.py:80
  8.1 1.4 %copy.47 = f32[32,65,64]{1,2,0:T(8,128)} copy(f32[32,65,64]{2,1,0:T(8,128)S(1)} %constant_dynamic-update-slice_fusion) | data formatting | bytes 1064960 | tf_op jit(solution)/shard_map/stack | solution.py:13
  9.5 7.5 %all-to-all-start = ((f32[32,65,64]{1,2,0:T(8,128)}), f32[32,65,64]{1,2,0:T(8,128)S(1)}, u32[]{:S(2)}, u32[]{:S(2)}) async-start(f32[32,65,64]{1,2,0:T(8,128)} %copy.47), calls=%async_computation | async-start | bytes 2097152 | tf_op jit(solution)/shard_map/all_to_all | solution.py:14
  17.0 0.3 reshape.138
  17.3 0.3 subtract_bitcast_fusion
  18.0 0.3 fusion.27
  18.3 26.1 %all-to-all-done = f32[32,65,64]{1,2,0:T(8,128)S(1)} async-done(((f32[32,65,64]{1,2,0:T(8,128)}), f32[32,65,64]{1,2,0:T(8,128)S(1)}, u32[]{:S(2)}, u32[]{:S(2)}) %all-to-all-start) | async-done | bytes 532512 | tf_op jit(solution)/shard_map/all_to_all | solution.py:14
  44.4 0.9 %fusion.30 = s32[32,64]{1,0:T(8,128)S(1)} fusion(f32[65,32,64]{0,2,1:T(8,128)S(1)} %bitcast.153), kind=kLoop, calls=%fused_computation.48 | loop fusion | flops 6144 | bytes 16384 | tf_op jit(solution)/shard_map/sub | solution.py:82
  45.4 2.2 %fusion.19 = f32[51,2048]{1,0:T(8,128)S(1)} fusion(s32[2048]{0:T(1024)S(1)} %sub.44, f32[48,512]{1,0:T(8,128)S(1)} %bitcast.162, f32[3,512]{1,0:T(4,128)S(1)} %copy-done.5), kind=kOutput, calls=%fused_computation.30 | convolution fusion | flops 642803200 | bytes 530432 | tf_op jit(solution)/shard_map/dot_general | solution.py:90
  47.7 0.7 copy-done.1
  48.4 0.9 %copy.48 = f32[64,32,64]{2,1,0:T(8,128)S(1)} copy(f32[64,32,64]{0,2,1:T(8,128)S(1)} %bitcast.154) | data formatting | bytes 1048576 | tf_op jit(solution)/shard_map/slice | solution.py:93
  49.3 0.4 reshape.137
  49.7 1.9 %convolution_bitcast_fusion = f32[4,64,2048]{2,1,0:T(8,128)S(1)} fusion(f32[4,16,2048]{2,1,0:T(8,128)S(1)} %reshape.137, f32[64,16]{0,1:T(8,128)S(1)} %copy-done), kind=kOutput, calls=%fused_computation.34 | convolution fusion | flops 100663296 | bytes 2625536 | tf_op jit(solution)/shard_map/jn,cns->cjs/dot_general | solution.py:94
  51.6 1.5 %multiply_reduce_fusion.1 = (f32[64,2048]{1,0:T(8,128)S(1)}, f32[3,64,2048]{2,1,0:T(8,128)}) fusion(f32[3,2048]{1,0:T(4,128)S(1)} %slice-done, f32[4,64,2048]{2,1,0:T(8,128)S(1)} %convolution_bitcast_fusion), kind=kLoop, calls=%fused_computation.40 | loop fusion | flops 1048576 | bytes 3694592 | tf_op jit(solution)/shard_map/reduce_sum | solution.py:30
  53.1 7.7 %multiply_reduce_fusion = f32[64,16,2048]{2,1,0:T(8,128)} fusion(f32[3,16,2048]{2,1,0:T(8,128)S(1)} %bitcast.156, f32[3,64,2048]{2,1,0:T(8,128)} %get-tuple-element.6), kind=kLoop, calls=%fused_computation.7 | loop fusion | flops 10485760 | bytes 10354688 | tf_op jit(solution)/shard_map/reduce_sum | solution.py:34
  61.0 14.1 %fusion.15 = f32[16,2048]{1,0:T(8,128)S(1)} fusion(f32[64,16,2048]{2,1,0:T(8,128)} %multiply_reduce_fusion, f32[16,2048]{1,0:T(8,128)S(1)} %multiply_reduce_fusion.2, f32[64,2048]{1,0:T(8,128)S(1)} %get-tuple-element.8, f32[64,2048]{1,0:T(8,128)S(1)} %get-tuple-element.7), kind=kLoop, calls=%fused_computation.24 | loop fusion | flops 96436224 | bytes 9699328 | tf_op jit(solution)/shard_map/reduce_sum | solution.py:44
  75.1 1.4 %fusion.18 = f32[16,512]{1,0:T(8,128)S(1)} fusion(s32[2048]{0:T(1024)S(1)} %sub.44, f32[16,2048]{1,0:T(8,128)S(1)} %fusion.15, pred[2048]{0:T(1024)(128)(4,1)S(1)} %broadcast_compare_fusion), kind=kOutput, calls=%fused_computation.29 | convolution fusion | flops 202407936 | bytes 174080 | tf_op jit(solution)/shard_map/dot_general | solution.py:98
  76.5 1.0 %fusion.24 = f32[1024,16]{1,0:T(8,128)S(1)} fusion(f32[16,512]{1,0:T(8,128)S(1)} %fusion.18, s32[512]{0:T(512)S(1)} %convert_add_fusion.1), kind=kOutput, calls=%fused_computation.38 | convolution fusion | flops 101187584 | bytes 100352 | tf_op jit(solution)/shard_map/dot_general | solution.py:104
  77.8 9.4 %all_to_all.15 = f32[32,1,512]{2,1,0:T(1,128)S(1)} all-to-all(f32[32,1,512]{2,1,0:T(1,128)S(1)} %all_to_all.12), channel_id=1, replica_groups=mesh['grp'=4,'dev'=8] {'grp','dev'}, dimensions={0} | all-to-all | bytes 131072 | tf_op jit(solution)/shard_map/all_to_all | solution.py:106
  87.2 0.6 copy.85
  (69 shorter events, 3.5 us)
Async XLA Ops:
  0.0 49.7 %copy-start = (f32[64,16]{0,1:T(8,128)S(1)}, f32[64,16]{0,1:T(8,128)}, u32[]{:S(2)}) copy-start(f32[64,16]{0,1:T(8,128)} %param.16) | copy-start | bytes 12292
  0.0 1.6 %copy-start.2 = (f32[3,8192]{1,0:T(4,128)S(1)}, f32[3,8192]{1,0:T(4,128)}, u32[]{:S(2)}) copy-start(f32[3,8192]{1,0:T(4,128)} %param.9) | copy-start | bytes 294916
  1.6 0.8 copy-start.4
  1.9 0.8 copy-start.6
  9.5 7.5 %copy-start.3 = (f32[3,8192]{1,0:T(4,128)S(1)}, f32[3,8192]{1,0:T(4,128)}, u32[]{:S(2)}) copy-start(f32[3,8192]{1,0:T(4,128)} %param.14) | copy-start | bytes 294916
  9.5 7.8 %copy-start.5 = (f32[3,512]{1,0:T(4,128)S(1)}, f32[3,512]{1,0:T(4,128)}, u32[]{:S(2)}) copy-start(f32[3,512]{1,0:T(4,128)} %param.13) | copy-start | bytes 18436
  9.5 34.9 %all-to-all-start = ((f32[32,65,64]{1,2,0:T(8,128)}), f32[32,65,64]{1,2,0:T(8,128)S(1)}, u32[]{:S(2)}, u32[]{:S(2)}) async-start(f32[32,65,64]{1,2,0:T(8,128)} %copy.47), calls=%async_computation | async-start | bytes 2097152 | tf_op jit(solution)/shard_map/all_to_all | solution.py:14
  17.3 0.7 copy-start.7
  47.6 0.8 copy-start.1
  49.7 1.9 %slice-start = ((f32[51,2048]{1,0:T(8,128)}), f32[3,2048]{1,0:T(4,128)S(1)}, s32[]{:S(2)}) async-start(f32[51,2048]{1,0:T(8,128)} %copy-done.1), calls=%async_computation.2 | async-start | bytes 65536 | tf_op jit(solution)/shard_map/slice | solution.py:91
  53.1 7.7 %copy-start.8 = (f32[64]{0:T(128)S(1)}, f32[64]{0:T(128)}, u32[]{:S(2)}) copy-start(f32[64]{0:T(128)} %param.17) | copy-start | bytes 772
